TPU v7x, 512 devices: a whole 4x8x8 slice. The times are simulated.
512 devices in a mesh: grp: 8 (over y_lo, core), own: 64 (over x, y_hi, z).
Axes of the slice: x: 4, y: 8 (y_hi: 2, y_lo: 4; y = y_hi * 4 + y_lo), z: 8, core: 2. Of those that a mesh axis runs over, the one named last changes fastest.
Arguments:
- activations: bfloat16 [65536, 1024], P(('grp', 'own'))
- out_grads: bfloat16 [65536, 1024], P(('grp', 'own')), may hold values from -0.01953125 to 0.01953125
- master: float32 [1024, 1024], P('own'), may hold values from -6 to 6
- moment: float32 [1024, 1024], P('own'), may hold values from 0.05 to 5
- left_root: bfloat16 [1024, 1024], P('own'), may hold values from -0.25 to 2.25, as said below
- right_root: bfloat16 [1024, 1024], P('own'), may hold values from -0.25 to 2.25, as said below
- stats_in: float32 [256, 16, 1024], P('own'), may hold values from -6 to 6
- tile_slot: int32 [128], replicated, may hold values from 0 to 255, as said below
Outputs:
- master_out: float32 [1024, 1024], P('own')
- moment_out: float32 [1024, 1024], P('own')
- stats_out: float32 [256, 16, 1024], P('own')
- weights: bfloat16 [1024, 1024], replicated
Inputs may be any that keep to these rules, and one draw needn't show every extreme that they name: `tile_slot`: distinct slot numbers; slot s belongs to owner s // 4; some owner holds 4 tiles. `left_root`: symmetric. `right_root`: symmetric.
All inputs are finite; a program needn't handle non-finite values.
Results may differ from a plain program's by a relative error of at most 0.005.
Values may be sent and summed in bfloat16 or wider, within the bound.
No kernel may reach another device: no remote copies, remote signals or barrier semaphores. Data moves between devices by JAX's collectives and lax.ppermute only.
A program may use at most 64 MiB of HBM per device.

v0:
```python
import jax
import jax.numpy as jnp
from jax import lax
from jax.sharding import Mesh
from jax.sharding import PartitionSpec as P

stat_decay = 0.9
moment_decay = 0.95
learn_rate = 0.3
adam_eps = 1e-08
norm_eps = 1e-06
GRP = ("yl", "c")
OWN = ("x", "yh", "z")
SUB_SIZES = (4, 2, 4, 2, 8)


def split3(value):
    hi = lax.reduce_precision(value, exponent_bits=8, mantissa_bits=7)
    rest = value - hi
    mid = lax.reduce_precision(rest, exponent_bits=8, mantissa_bits=7)
    lo = lax.reduce_precision(rest - mid, exponent_bits=8, mantissa_bits=7)
    return jnp.stack([hi, mid, lo])


def gather_own_rows(block):
    rows = block.shape[0]
    out = block
    for axis in ("yh", "x", "z"):
        out = lax.all_gather(out, axis, axis=0, tiled=True)
    out = out.reshape(SUB_SIZES[4], SUB_SIZES[2], SUB_SIZES[3], rows, block.shape[1])
    out = jnp.transpose(out, (1, 2, 0, 3, 4))
    return out.reshape(-1, block.shape[1])


def local(activations, out_grads, master, moment, left_root, right_root, stats_in, tile_slot):
    owner_rows = master.shape[0]
    block_size = master.shape[1]
    owners = block_size // owner_rows
    capacity = stats_in.shape[0]
    tile_rows = stats_in.shape[1]
    tile_count = tile_slot.shape[0]
    owner_index = lax.axis_index(OWN)
    grp_size = SUB_SIZES[0] * SUB_SIZES[1]
    right_full = gather_own_rows(right_root)
    partial = lax.dot_general(
        activations, out_grads, (((0,), (0,)), ((), ())), preferred_element_type=jnp.float32
    )
    pieces = lax.all_to_all(partial.reshape(owners, owner_rows, block_size), OWN, 0, 0, tiled=True)
    own_sum = jnp.sum(pieces, axis=0)
    copies = jnp.broadcast_to(own_sum[None], (grp_size, owner_rows, block_size))
    grad_rows = jnp.sum(lax.all_to_all(copies, GRP, 0, 0, tiled=True), axis=0)
    moment_out = moment_decay * moment + (1.0 - moment_decay) * grad_rows * grad_rows
    adam_dir = grad_rows / (jnp.sqrt(moment_out) + adam_eps)
    adam_part = split3(jnp.sum(adam_dir * adam_dir))
    extra = jnp.zeros((1, block_size), jnp.float32).at[0, :3].set(adam_part)
    payload = jnp.concatenate([grad_rows, extra], axis=0).astype(jnp.bfloat16)
    sent = jnp.broadcast_to(payload[None], (owners,) + payload.shape)
    got = lax.all_to_all(sent, OWN, 0, 0, tiled=True)
    grad_low = got[:, :owner_rows, :].reshape(block_size, block_size)
    adam_sum = jnp.sum(got[:, owner_rows, :3].astype(jnp.float32))
    left_mid = jnp.dot(left_root, grad_low, preferred_element_type=jnp.float32).astype(jnp.bfloat16)
    precond = jnp.dot(left_mid, right_full, preferred_element_type=jnp.float32)
    precond_part = jnp.broadcast_to(jnp.sum(precond * precond), (owners, 1, 128))
    precond_sum = jnp.sum(lax.all_to_all(precond_part, OWN, 0, 0, tiled=True)[:, 0, 0])
    graft_scale = jnp.sqrt(adam_sum) / (jnp.sqrt(precond_sum) + norm_eps)
    master_out = master - learn_rate * graft_scale * precond
    weight_rows = jnp.broadcast_to(
        master_out.astype(jnp.bfloat16)[None], (owners, owner_rows, block_size)
    )
    weights = lax.all_to_all(weight_rows, OWN, 0, 0, tiled=True).reshape(block_size, block_size)
    my_slots = owner_index * capacity + jnp.arange(capacity, dtype=jnp.int32)
    matches = (tile_slot[:, None] == my_slots[None, :]).astype(jnp.int32)
    tile_ids = jnp.sum(matches * jnp.arange(tile_count, dtype=jnp.int32)[:, None], axis=0)
    filled = jnp.sum(matches, axis=0)
    per_half = block_size // tile_rows
    which_half = tile_ids // per_half
    offsets = (tile_ids - which_half * per_half) * tile_rows
    grad_low_t = grad_low.T
    row_blocks = jnp.concatenate(
        [lax.dynamic_slice_in_dim(grad_low, offsets[s], tile_rows, 0) for s in range(capacity)],
        axis=0,
    )
    col_blocks = jnp.concatenate(
        [lax.dynamic_slice_in_dim(grad_low_t, offsets[s], tile_rows, 0) for s in range(capacity)],
        axis=0,
    )
    left_tiles = lax.dot_general(
        row_blocks, grad_low, (((1,), (1,)), ((), ())), preferred_element_type=jnp.float32
    ).reshape(capacity, tile_rows, block_size)
    right_tiles = jnp.dot(col_blocks, grad_low, preferred_element_type=jnp.float32).reshape(
        capacity, tile_rows, block_size
    )
    product = jnp.where((which_half == 0)[:, None, None], left_tiles, right_tiles)
    fresh = stat_decay * stats_in + (1.0 - stat_decay) / block_size * product
    stats_out = jnp.where((filled > 0)[:, None, None], fresh, 0.0)
    return (master_out, moment_out, stats_out, weights)


def solution(mesh):
    sub_mesh = Mesh(mesh.devices.reshape(SUB_SIZES), GRP + OWN)
    rows_all = P(GRP + OWN, None)
    rows_own = P(OWN, None)
    in_specs = (rows_all, rows_all, rows_own, rows_own, rows_own, rows_own, P(OWN, None, None), P())
    out_specs = (rows_own, rows_own, P(OWN, None, None), P())
    return jax.shard_map(
        local, mesh=sub_mesh, in_specs=in_specs, out_specs=out_specs, check_vma=False
    )
```

profile of v0, /device:TPU:8, one launch (start us, length us, event | category | flops | bytes accessed | tf_op | source)
XLA Modules:
  0.0 407.6 jit_solution(5947708179712578350)
XLA Ops:
  7.2 0.0 copy-start
  7.2 0.9 copy-done
  8.1 1.7 fusion.12
  9.8 122.6 %all_to_all.25 = f32[64,16,1024]{2,1,0:T(8,128)} all-to-all(f32[64,16,1024]{2,1,0:T(8,128)S(1)} %bitcast.42), channel_id=1, replica_groups=mesh['yl'=4,'c'=2,'x'=4,'yh'=2,'z'=8] {'x','yh','z'}, dimensions={0} | all-to-all | bytes 8388608 | tf_op jit(solution)/shard_map/all_to_all | solution.py:48
  132.4 2.4 reduce_sum.72
  134.8 0.0 copy-start.2
  134.8 0.8 broadcast_in_dim.24
  135.6 3.4 all-to-all-start.1
  139.1 0.6 compare_reduce_fusion
  139.7 11.3 %all-to-all-done.1 = f32[8,16,1024]{2,1,0:T(8,128)S(1)} async-done(((f32[8,16,1024]{2,1,0:T(8,128)}), f32[8,16,1024]{2,1,0:T(8,128)S(1)}, u32[]{:S(2)}, u32[]{:S(2)}) %all-to-all-start.1) | async-done | bytes 524320 | tf_op jit(solution)/shard_map/all_to_all | solution.py:51
  151.1 0.0 copy-done.2
  151.1 1.3 multiply_reduce_fusion.1
  156.5 2.7 fusion.8
  159.3 2.1 broadcast_in_dim.25
  161.4 6.8 %all-to-all-start.2 = ((bf16[64,17,1024]{2,1,0:T(8,128)(2,1)}), bf16[64,17,1024]{2,1,0:T(8,128)(2,1)}, u32[]{:S(2)}, u32[]{:S(2)}) async-start(bf16[64,17,1024]{2,1,0:T(8,128)(2,1)} %broadcast_in_dim.25), calls=%async_computation.2 | async-start | bytes 6291456 | tf_op jit(solution)/shard_map/all_to_all | solution.py:58
  168.2 0.0 all-gather.2.cloned.1.call-start
  168.3 0.0 copy-done.5
  168.3 53.6 %all_gather.9 = bf16[32,1024]{1,0:T(8,128)(2,1)S(1)} all-gather(bf16[16,1024]{1,0:T(8,128)(2,1)S(1)} %copy-done.5), channel_id=1, replica_groups=mesh['yl'=4,'c'=2,'x'=4,'yh'=2,'z'=8] {'yh'}, dimensions={0}, use_global_device_ids=true | all-gather | bytes 98304 | tf_op jit(solution)/shard_map/all_gather | solution.py:29
  221.9 19.4 %all_gather.10 = bf16[128,1024]{1,0:T(8,128)(2,1)} all-gather(bf16[32,1024]{1,0:T(8,128)(2,1)S(1)} %all_gather.9), channel_id=1, replica_groups=mesh['yl'=4,'c'=2,'x'=4,'yh'=2,'z'=8] {'x'}, dimensions={0}, use_global_device_ids=true | all-gather | bytes 327680 | tf_op jit(solution)/shard_map/all_gather | solution.py:29
  241.3 0.0 all-gather.2.cloned.1.call-update
  241.3 58.9 %all-gather.2.cloned.1.call-done = bf16[1024,1024]{1,0:T(8,128)(2,1)} async-done(((bf16[128,1024]{1,0:T(8,128)(2,1)}), bf16[1024,1024]{1,0:T(8,128)(2,1)}) %all-gather.2.cloned.1.call-update) | async-done | bytes 2097168 | tf_op jit(solution)/shard_map/all_gather | solution.py:29
  300.2 3.2 copy.18
  303.4 0.0 all-to-all-done.2
  303.4 1.9 slice.49
  305.3 0.0 copy-done.4
  305.3 0.0 copy-start.3
  305.3 2.9 multiply_reduce_fusion
  308.2 1.3 broadcast_in_dim.26
  309.5 11.8 %all-to-all-start.3 = ((f32[64,1,128]{2,1,0:T(1,128)}), f32[64,1,128]{2,1,0:T(1,128)S(1)}, u32[]{:S(2)}, u32[]{:S(2)}) async-start(f32[64,1,128]{2,1,0:T(1,128)} %broadcast_in_dim.26), calls=%async_computation.3 | async-start | bytes 65536 | tf_op jit(solution)/shard_map/all_to_all | solution.py:64
  321.3 1.6 fusion.5
  323.6 12.0 %all-to-all-done.3 = f32[64,1,128]{2,1,0:T(1,128)S(1)} async-done(((f32[64,1,128]{2,1,0:T(1,128)}), f32[64,1,128]{2,1,0:T(1,128)S(1)}, u32[]{:S(2)}, u32[]{:S(2)}) %all-to-all-start.3) | async-done | bytes 32800 | tf_op jit(solution)/shard_map/all_to_all | solution.py:64
  335.5 0.7 slice_reduce_fusion
  336.9 0.0 copy-done.3
  337.0 0.6 fusion.9
  337.6 1.6 broadcast_in_dim.53
  339.2 5.7 %all-to-all-start.4 = ((bf16[64,16,1024]{2,1,0:T(8,128)(2,1)}), bf16[64,16,1024]{2,1,0:T(8,128)(2,1)}, u32[]{:S(2)}, u32[]{:S(2)}) async-start(bf16[64,16,1024]{2,1,0:T(8,128)(2,1)} %broadcast_in_dim.53), calls=%async_computation.4 | async-start | bytes 4194304 | tf_op jit(solution)/shard_map/all_to_all | solution.py:70
  344.9 0.0 copy-done.6
  344.9 0.2 fusion.6
  345.1 0.6 fusion.11
  353.2 0.4 dynamic-slice_bitcast_fusion.3
  353.7 0.0 copy-start.1
  353.7 0.4 pad_maximum_fusion
  354.0 0.1 copy.20
  354.2 0.1 constant_dynamic-slice_fusion.3
  354.2 0.8 fusion.13
  355.0 1.2 fusion.2
  356.2 41.4 %all-to-all-done.4 = bf16[64,16,1024]{2,1,0:T(8,128)(2,1)} async-done(((bf16[64,16,1024]{2,1,0:T(8,128)(2,1)}), bf16[64,16,1024]{2,1,0:T(8,128)(2,1)}, u32[]{:S(2)}, u32[]{:S(2)}) %all-to-all-start.4) | async-done | bytes 2097184 | tf_op jit(solution)/shard_map/all_to_all | solution.py:70
  397.7 3.1 copy.23
  (12 shorter events, 0.1 us)
Async XLA Ops:
  7.2 1.0 copy-start
  134.8 16.3 %copy-start.2 = (f32[16,1024]{1,0:T(8,128)S(1)}, f32[16,1024]{1,0:T(8,128)}, u32[]{:S(2)}) copy-start(f32[16,1024]{1,0:T(8,128)} %param.13) | copy-start | bytes 196612
  135.6 15.4 %all-to-all-start.1 = ((f32[8,16,1024]{2,1,0:T(8,128)}), f32[8,16,1024]{2,1,0:T(8,128)S(1)}, u32[]{:S(2)}, u32[]{:S(2)}) async-start(f32[8,16,1024]{2,1,0:T(8,128)} %broadcast_in_dim.24), calls=%async_computation.1 | async-start | bytes 1048576 | tf_op jit(solution)/shard_map/all_to_all | solution.py:51
  161.4 6.9 %copy-start.5 = (bf16[16,1024]{1,0:T(8,128)(2,1)S(1)}, bf16[16,1024]{1,0:T(8,128)(2,1)}, u32[]{:S(2)}) copy-start(bf16[16,1024]{1,0:T(8,128)(2,1)} %param.15) | copy-start | bytes 98308
  161.4 142.0 %all-to-all-start.2 = ((bf16[64,17,1024]{2,1,0:T(8,128)(2,1)}), bf16[64,17,1024]{2,1,0:T(8,128)(2,1)}, u32[]{:S(2)}, u32[]{:S(2)}) async-start(bf16[64,17,1024]{2,1,0:T(8,128)(2,1)} %broadcast_in_dim.25), calls=%async_computation.2 | async-start | bytes 6291456 | tf_op jit(solution)/shard_map/all_to_all | solution.py:58
  168.2 132.0 %all-gather.2.cloned.1.call-start = ((), (), s32[]{:S(2)}) async-start(), calls=%async_computation.5 | async-start | bytes 2359296 | tf_op jit(solution)/shard_map/all_gather | solution.py:29
  303.4 1.9 copy-start.4
  305.3 31.6 %copy-start.3 = (f32[16,1024]{1,0:T(8,128)S(1)}, f32[16,1024]{1,0:T(8,128)}, u32[]{:S(2)}) copy-start(f32[16,1024]{1,0:T(8,128)} %param.12) | copy-start | bytes 196612
  309.5 26.0 %all-to-all-start.3 = ((f32[64,1,128]{2,1,0:T(1,128)}), f32[64,1,128]{2,1,0:T(1,128)S(1)}, u32[]{:S(2)}, u32[]{:S(2)}) async-start(f32[64,1,128]{2,1,0:T(1,128)} %broadcast_in_dim.26), calls=%async_computation.3 | async-start | bytes 65536 | tf_op jit(solution)/shard_map/all_to_all | solution.py:64
  339.2 5.7 %copy-start.6 = (s32[128]{0:T(128)S(1)}, s32[128]{0:T(128)}, u32[]{:S(2)}) copy-start(s32[128]{0:T(128)} %param.17) | copy-start | bytes 1540
  339.2 58.5 %all-to-all-start.4 = ((bf16[64,16,1024]{2,1,0:T(8,128)(2,1)}), bf16[64,16,1024]{2,1,0:T(8,128)(2,1)}, u32[]{:S(2)}, u32[]{:S(2)}) async-start(bf16[64,16,1024]{2,1,0:T(8,128)(2,1)} %broadcast_in_dim.53), calls=%async_computation.4 | async-start | bytes 4194304 | tf_op jit(solution)/shard_map/all_to_all | solution.py:70
  353.7 1.3 copy-start.1
Sparse Core Ops, SparseCore 0:
  241.4 58.7 all-gather.1
where the time goes:
time: 409 us; the launch traced here: 408 us
  blocking collectives  196 us (48%)
  waiting for transfers between devices  124 us (30%)
  starting transfers between devices  27.8 us (7%)
  between operations  27.3 us (7%)
  local copies, waits for them, and re-layouts  16.2 us (4%)
  other arithmetic  10.5 us (3%)
  matrix products  6.56 us (2%)
    all_to_all x1, blocking collectives, local(): lax.all_to_all(partial.reshape(owners, owner_rows, block_size), OWN, 0, 0...  123 us
    all_gather x2, blocking collectives, gather_own_rows(): out = lax.all_gather(out, axis, axis=0, tiled=True)  73 us
    all_gather x1, waiting for transfers between devices, gather_own_rows(): out = lax.all_gather(out, axis, axis=0, tiled=True)  58.9 us
    all_to_all x1, waiting for transfers between devices, local(): lax.all_to_all(weight_rows, OWN, 0, 0, tiled=True)  41.4 us
    all_to_all x1, waiting for transfers between devices, local(): lax.all_to_all(precond_part, OWN, 0, 0, tiled=True)[:, 0, 0]  12 us
    all_to_all x1, starting transfers between devices, local(): lax.all_to_all(precond_part, OWN, 0, 0, tiled=True)[:, 0, 0]  11.8 us
    all_to_all x1, waiting for transfers between devices, local(): grad_rows = jnp.sum(lax.all_to_all(copies, GRP, 0, 0, tiled=True), axis=0)  11.3 us
  transfers between devices with their start and end apart: 5, of which 4 were waited for; matrix products, arithmetic and copies ran while one was open for 2% of the time, Pallas kernels for 0%

commit v1 on v0

--- a/solution.py
+++ b/solution.py
@@ -26,7 +26,14 @@
     rows = block.shape[0]
     out = block
     for axis in ("yh", "x", "z"):
-        out = lax.all_gather(out, axis, axis=0, tiled=True)
+
+        def views_find(shard_in, link_axis):
+            mid_arr = jnp.stack(lax.axis_size(link_axis) * [shard_in])
+            aux = lax.all_to_all(mid_arr, axis_name=link_axis, split_axis=0, concat_axis=0)
+            step_out = jnp.concatenate(aux, axis=0)
+            return step_out
+
+        out = views_find(out, axis)
     out = out.reshape(SUB_SIZES[4], SUB_SIZES[2], SUB_SIZES[3], rows, block.shape[1])
     out = jnp.transpose(out, (1, 2, 0, 3, 4))
     return out.reshape(-1, block.shape[1])

time: 409 us -> 399 us (0.976)
  the two profiles are of different devices: /device:TPU:8 before, /device:TPU:2 now
where the time goes in v1:
time: 399 us; the launch traced here: 398 us
  waiting for transfers between devices  175 us (44%)
  blocking collectives  135 us (34%)
  starting transfers between devices  38.8 us (10%)
  local copies, waits for them, and re-layouts  15.2 us (4%)
  between operations  13.9 us (3%)
  other arithmetic  11.9 us (3%)
  matrix products  8.48 us (2%)
    all_to_all x1, blocking collectives, local(): lax.all_to_all(partial.reshape(owners, owner_rows, block_size), OWN, 0, 0...  114 us
    all_to_all x1, waiting for transfers between devices, local(): got = lax.all_to_all(sent, OWN, 0, 0, tiled=True)  74.6 us
    all_to_all x3, waiting for transfers between devices, views_find(): lax.all_to_all(mid_arr, axis_name=link_axis, split_axis=0, concat_axis=0)  49.5 us
    all_to_all x1, waiting for transfers between devices, local(): lax.all_to_all(weight_rows, OWN, 0, 0, tiled=True)  39.7 us
    all_to_all x1, blocking collectives, local(): grad_rows = jnp.sum(lax.all_to_all(copies, GRP, 0, 0, tiled=True), axis=0)  20.6 us
    all_to_all x3, starting transfers between devices, views_find(): lax.all_to_all(mid_arr, axis_name=link_axis, split_axis=0, concat_axis=0)  15.6 us
    all_to_all x1, waiting for transfers between devices, local(): lax.all_to_all(precond_part, OWN, 0, 0, tiled=True)[:, 0, 0]  11 us
    all_to_all x1, starting transfers between devices, local(): lax.all_to_all(precond_part, OWN, 0, 0, tiled=True)[:, 0, 0]  10.2 us
  transfers between devices with their start and end apart: 6, of which 6 were waited for; matrix products, arithmetic and copies ran while one was open for 4% of the time, Pallas kernels for 0%

profile of v1, /device:TPU:2, one launch (start us, length us, event | category | flops | bytes accessed | tf_op | source)
XLA Modules:
  0.0 398.2 jit_solution(1630914862766963918)
XLA Ops:
  0.6 0.0 copy-start
  0.6 1.5 pad_maximum_fusion.2
  2.1 7.1 %all-to-all-start.3 = ((bf16[2,16,1024]{2,1,0:T(8,128)(2,1)}), bf16[2,16,1024]{2,1,0:T(8,128)(2,1)S(1)}, u32[]{:S(2)}, u32[]{:S(2)}) async-start(bf16[2,16,1024]{2,1,0:T(8,128)(2,1)} %pad_maximum_fusion.2), calls=%async_computation.3 | async-start | bytes 131072 | tf_op jit(solution)/shard_map/all_to_all | solution.py:32
  9.2 0.0 copy-done
  9.2 3.6 fusion.12
  12.8 4.4 %all-to-all-done.3 = bf16[2,16,1024]{2,1,0:T(8,128)(2,1)S(1)} async-done(((bf16[2,16,1024]{2,1,0:T(8,128)(2,1)}), bf16[2,16,1024]{2,1,0:T(8,128)(2,1)S(1)}, u32[]{:S(2)}, u32[]{:S(2)}) %all-to-all-start.3) | async-done | bytes 65568 | tf_op jit(solution)/shard_map/all_to_all | solution.py:32
  17.2 114.4 %all_to_all.40 = f32[64,16,1024]{2,1,0:T(8,128)} all-to-all(f32[64,16,1024]{2,1,0:T(8,128)} %bitcast.45), channel_id=1, replica_groups=mesh['yl'=4,'c'=2,'x'=4,'yh'=2,'z'=8] {'x','yh','z'}, dimensions={0} | all-to-all | bytes 8388608 | tf_op jit(solution)/shard_map/all_to_all | solution.py:55
  131.7 0.7 stack.31
  132.4 4.7 %all-to-all-start.4 = ((bf16[4,32,1024]{2,1,0:T(8,128)(2,1)}), bf16[4,32,1024]{2,1,0:T(8,128)(2,1)S(1)}, u32[]{:S(2)}, u32[]{:S(2)}) async-start(bf16[4,32,1024]{2,1,0:T(8,128)(2,1)} %stack.31), calls=%async_computation.4 | async-start | bytes 524288 | tf_op jit(solution)/shard_map/all_to_all | solution.py:32
  137.1 2.4 reduce_sum.72
  139.5 2.8 all-to-all-done.4
  142.4 20.6 %all_to_all.41 = f32[8,16,1024]{2,1,0:T(8,128)S(1)} all-to-all(f32[8,16,1024]{2,1,0:T(8,128)S(1)} %broadcast_in_dim.24), channel_id=1, replica_groups=mesh['yl'=4,'c'=2,'x'=4,'yh'=2,'z'=8] {'yl','c'}, dimensions={0} | all-to-all | bytes 1048576 | tf_op jit(solution)/shard_map/all_to_all | solution.py:58
  163.0 1.6 stack.32
  164.6 3.7 all-to-all-start.5
  168.4 0.6 compare_reduce_fusion
  169.0 0.0 copy-done.2
  169.0 1.3 multiply_reduce_fusion.1
  174.5 2.6 fusion.8
  177.2 42.2 %all-to-all-done.5 = bf16[8,128,1024]{2,1,0:T(8,128)(2,1)S(1)} async-done(((bf16[8,128,1024]{2,1,0:T(8,128)(2,1)}), bf16[8,128,1024]{2,1,0:T(8,128)(2,1)S(1)}, u32[]{:S(2)}, u32[]{:S(2)}) %all-to-all-start.5) | async-done | bytes 2097184 | tf_op jit(solution)/shard_map/all_to_all | solution.py:32
  219.4 2.1 broadcast_in_dim.25
  221.5 6.5 %all-to-all-start.2 = ((bf16[64,17,1024]{2,1,0:T(8,128)(2,1)}), bf16[64,17,1024]{2,1,0:T(8,128)(2,1)}, u32[]{:S(2)}, u32[]{:S(2)}) async-start(bf16[64,17,1024]{2,1,0:T(8,128)(2,1)} %broadcast_in_dim.25), calls=%async_computation.2 | async-start | bytes 6291456 | tf_op jit(solution)/shard_map/all_to_all | solution.py:65
  228.0 1.6 copy.18
  229.6 74.6 %all-to-all-done.2 = bf16[64,17,1024]{2,1,0:T(8,128)(2,1)} async-done(((bf16[64,17,1024]{2,1,0:T(8,128)(2,1)}), bf16[64,17,1024]{2,1,0:T(8,128)(2,1)}, u32[]{:S(2)}, u32[]{:S(2)}) %all-to-all-start.2) | async-done | bytes 2228256 | tf_op jit(solution)/shard_map/all_to_all | solution.py:65
  304.3 1.9 slice.49
  306.2 0.0 copy-done.4
  306.2 0.0 copy-start.3
  306.2 2.9 multiply_reduce_fusion
  309.1 1.3 broadcast_in_dim.26
  310.4 10.2 %all-to-all-start.6 = ((f32[64,1,128]{2,1,0:T(1,128)}), f32[64,1,128]{2,1,0:T(1,128)S(1)}, u32[]{:S(2)}, u32[]{:S(2)}) async-start(f32[64,1,128]{2,1,0:T(1,128)} %broadcast_in_dim.26), calls=%async_computation.6 | async-start | bytes 65536 | tf_op jit(solution)/shard_map/all_to_all | solution.py:71
  320.6 1.6 fusion.5
  322.8 11.0 %all-to-all-done.6 = f32[64,1,128]{2,1,0:T(1,128)S(1)} async-done(((f32[64,1,128]{2,1,0:T(1,128)}), f32[64,1,128]{2,1,0:T(1,128)S(1)}, u32[]{:S(2)}, u32[]{:S(2)}) %all-to-all-start.6) | async-done | bytes 32800 | tf_op jit(solution)/shard_map/all_to_all | solution.py:71
  333.8 0.7 slice_reduce_fusion
  335.2 0.0 copy-done.3
  335.3 0.6 fusion.9
  335.9 1.6 broadcast_in_dim.53
  337.5 6.6 %all-to-all-start.7 = ((bf16[64,16,1024]{2,1,0:T(8,128)(2,1)}), bf16[64,16,1024]{2,1,0:T(8,128)(2,1)}, u32[]{:S(2)}, u32[]{:S(2)}) async-start(bf16[64,16,1024]{2,1,0:T(8,128)(2,1)} %broadcast_in_dim.53), calls=%async_computation.7 | async-start | bytes 4194304 | tf_op jit(solution)/shard_map/all_to_all | solution.py:77
  344.1 0.2 fusion.6
  344.3 0.6 fusion.11
  352.4 0.5 dynamic-slice_bitcast_fusion.3
  352.9 0.0 copy-start.1
  352.9 0.4 pad_maximum_fusion
  353.2 0.1 copy.20
  353.4 0.1 constant_dynamic-slice_fusion.3
  353.4 0.8 fusion.13
  354.2 0.0 copy-done.1
  354.2 1.2 fusion.2
  355.4 39.7 %all-to-all-done.7 = bf16[64,16,1024]{2,1,0:T(8,128)(2,1)} async-done(((bf16[64,16,1024]{2,1,0:T(8,128)(2,1)}), bf16[64,16,1024]{2,1,0:T(8,128)(2,1)}, u32[]{:S(2)}, u32[]{:S(2)}) %all-to-all-start.7) | async-done | bytes 2097184 | tf_op jit(solution)/shard_map/all_to_all | solution.py:77
  395.1 3.1 copy.23
  (13 shorter events, 0.1 us)
Async XLA Ops:
  0.6 8.6 %copy-start = (bf16[128,1024]{1,0:T(8,128)(2,1)S(1)}, bf16[128,1024]{1,0:T(8,128)(2,1)}, u32[]{:S(2)}) copy-start(bf16[128,1024]{1,0:T(8,128)(2,1)} %param.10) | copy-start | bytes 786436
  2.1 15.1 %all-to-all-start.3 = ((bf16[2,16,1024]{2,1,0:T(8,128)(2,1)}), bf16[2,16,1024]{2,1,0:T(8,128)(2,1)S(1)}, u32[]{:S(2)}, u32[]{:S(2)}) async-start(bf16[2,16,1024]{2,1,0:T(8,128)(2,1)} %pad_maximum_fusion.2), calls=%async_computation.3 | async-start | bytes 131072 | tf_op jit(solution)/shard_map/all_to_all | solution.py:32
  132.4 10.0 %all-to-all-start.4 = ((bf16[4,32,1024]{2,1,0:T(8,128)(2,1)}), bf16[4,32,1024]{2,1,0:T(8,128)(2,1)S(1)}, u32[]{:S(2)}, u32[]{:S(2)}) async-start(bf16[4,32,1024]{2,1,0:T(8,128)(2,1)} %stack.31), calls=%async_computation.4 | async-start | bytes 524288 | tf_op jit(solution)/shard_map/all_to_all | solution.py:32
  164.6 4.4 %copy-start.2 = (f32[16,1024]{1,0:T(8,128)S(1)}, f32[16,1024]{1,0:T(8,128)}, u32[]{:S(2)}) copy-start(f32[16,1024]{1,0:T(8,128)} %param.13) | copy-start | bytes 196612
  164.6 54.8 %all-to-all-start.5 = ((bf16[8,128,1024]{2,1,0:T(8,128)(2,1)}), bf16[8,128,1024]{2,1,0:T(8,128)(2,1)S(1)}, u32[]{:S(2)}, u32[]{:S(2)}) async-start(bf16[8,128,1024]{2,1,0:T(8,128)(2,1)} %stack.32), calls=%async_computation.5 | async-start | bytes 4194304 | tf_op jit(solution)/shard_map/all_to_all | solution.py:32
  221.5 82.8 %all-to-all-start.2 = ((bf16[64,17,1024]{2,1,0:T(8,128)(2,1)}), bf16[64,17,1024]{2,1,0:T(8,128)(2,1)}, u32[]{:S(2)}, u32[]{:S(2)}) async-start(bf16[64,17,1024]{2,1,0:T(8,128)(2,1)} %broadcast_in_dim.25), calls=%async_computation.2 | async-start | bytes 6291456 | tf_op jit(solution)/shard_map/all_to_all | solution.py:65
  229.6 76.5 %copy-start.4 = (bf16[16,1024]{1,0:T(8,128)(2,1)S(1)}, bf16[16,1024]{1,0:T(8,128)(2,1)}, u32[]{:S(2)}) copy-start(bf16[16,1024]{1,0:T(8,128)(2,1)} %param.14) | copy-start | bytes 98308
  306.2 29.1 %copy-start.3 = (f32[16,1024]{1,0:T(8,128)S(1)}, f32[16,1024]{1,0:T(8,128)}, u32[]{:S(2)}) copy-start(f32[16,1024]{1,0:T(8,128)} %param.12) | copy-start | bytes 196612
  310.4 23.5 %all-to-all-start.6 = ((f32[64,1,128]{2,1,0:T(1,128)}), f32[64,1,128]{2,1,0:T(1,128)S(1)}, u32[]{:S(2)}, u32[]{:S(2)}) async-start(f32[64,1,128]{2,1,0:T(1,128)} %broadcast_in_dim.26), calls=%async_computation.6 | async-start | bytes 65536 | tf_op jit(solution)/shard_map/all_to_all | solution.py:71
  337.5 6.6 %copy-start.5 = (s32[128]{0:T(128)S(1)}, s32[128]{0:T(128)}, u32[]{:S(2)}) copy-start(s32[128]{0:T(128)} %param.17) | copy-start | bytes 1540
  337.5 57.7 %all-to-all-start.7 = ((bf16[64,16,1024]{2,1,0:T(8,128)(2,1)}), bf16[64,16,1024]{2,1,0:T(8,128)(2,1)}, u32[]{:S(2)}, u32[]{:S(2)}) async-start(bf16[64,16,1024]{2,1,0:T(8,128)(2,1)} %broadcast_in_dim.53), calls=%async_computation.7 | async-start | bytes 4194304 | tf_op jit(solution)/shard_map/all_to_all | solution.py:77
  352.9 1.3 copy-start.1
